TPU v7x, 128 devices: a whole 4x4x4 slice. The times are simulated.
128 devices in a mesh: chan: 32 (over x, y_lo, z), blk: 4 (over y_hi, core).
Axes of the slice: x: 4, y: 4 (y_hi: 2, y_lo: 2; y = y_hi * 2 + y_lo), z: 4, core: 2. Of those that a mesh axis runs over, the one named last changes fastest.
Arguments:
- voltages: int32 [2048, 134656], P(('chan', 'blk')), may hold values from -128 to 127
- flags: int32 [2048], P(('chan', 'blk')), may hold values 0 or 1
- model_amp: float32 [128, 2048], P('chan'), may hold values from 0.04 to 0.4
- model_phase: float32 [128, 2048], P('chan'), may hold values from -3.140625 to 3.140625
Outputs:
- visibility: bfloat16 [2, 128, 2048, 2048], P(None, 'chan', 'blk')
- gains: float32 [2, 128, 2048], P(None, None, ('chan', 'blk'))
All inputs are finite; a program needn't handle non-finite values. No bound on the sum of `flags` on one device may be relied on, other than what follows from the above.
Results may differ from a plain program's by a relative error of at most 0.0091.
Values may be sent and summed in bfloat16 or wider, within the bound.
No kernel may reach another device: no remote copies, remote signals or barrier semaphores. Data moves between devices by JAX's collectives and lax.ppermute only.
A program may use at most 256 MiB of HBM per device.

v0:
```python
import math
import jax
import jax.numpy as jnp
from jax import lax
from jax.sharding import PartitionSpec as P

CHANS = 128
FRAME = 512
TAPS = 8
BAND_START = 64
SPECTRA = 256
ITERS = 10


def window_table():
    index = jnp.arange(TAPS * FRAME, dtype=jnp.float32)
    offset = (index - TAPS * FRAME / 2 + 0.5) / FRAME
    taper = 0.5 - 0.5 * jnp.cos(2.0 * math.pi * (index + 0.5) / (TAPS * FRAME))
    return (jnp.sinc(offset) * taper).reshape(TAPS, FRAME)


def transform_table():
    sample = jnp.arange(FRAME, dtype=jnp.int32)
    channel = BAND_START + jnp.arange(CHANS, dtype=jnp.int32)
    angle = (sample[:, None] * channel[None, :] % FRAME).astype(jnp.float32) * (
        2.0 * math.pi / FRAME
    )
    return jnp.stack([jnp.cos(angle), -jnp.sin(angle)], axis=1).astype(jnp.bfloat16)


def channelize(voltages, keep):
    window = window_table()
    table = transform_table()
    count = voltages.shape[0]
    samples = voltages.astype(jnp.float32).reshape(count, SPECTRA + TAPS - 1, FRAME)
    frames = window[0] * samples[:, 0:SPECTRA, :]
    for tap in range(1, TAPS):
        frames = frames + window[tap] * samples[:, tap : tap + SPECTRA, :]
    frames = frames.astype(jnp.bfloat16)
    spectra = jnp.einsum("itj,jrc->cirt", frames, table, preferred_element_type=jnp.float32)
    scale = 1.0 / (64.0 * math.sqrt(FRAME))
    return (spectra * (scale * keep)[None, :, None, None]).astype(jnp.bfloat16)


def update_gains(model_re, model_im, power, product_re, product_im):
    denominator = (model_re * model_re + model_im * model_im) * (power[:, None] + 1e-06)
    new_re = (model_re * product_re + model_im * product_im) / denominator
    new_im = (model_re * product_im - model_im * product_re) / denominator
    return (new_re, new_im)


def shards(voltages, flags, model_amp, model_phase):
    keep = (1 - flags).astype(jnp.float32)
    input_count = voltages.shape[0]
    spectra = channelize(voltages, keep)
    blk_count = lax.axis_size("blk")
    block_index = lax.axis_index("blk")
    grouped = lax.all_gather(spectra, "blk", axis=1, tiled=True)
    turned = lax.all_to_all(grouped, "chan", split_axis=0, concat_axis=1, tiled=True)
    local_chans = turned.shape[0]
    all_inputs = turned.shape[1]
    row_count = all_inputs // blk_count
    whole = turned.reshape(local_chans, all_inputs, 2 * SPECTRA)
    rows = lax.dynamic_slice_in_dim(whole, block_index * row_count, row_count, 1)
    rotated = jnp.concatenate([rows[:, :, SPECTRA:], -rows[:, :, :SPECTRA]], axis=2)
    stacked = jnp.stack([rows, rotated])
    correlation = (
        jnp.einsum("rcpk,cqk->rcpq", stacked, whole, preferred_element_type=jnp.float32) / SPECTRA
    )
    visibility = correlation.astype(jnp.bfloat16)
    high = lax.Precision.HIGHEST
    full_re = model_amp * jnp.cos(model_phase)
    full_im = model_amp * jnp.sin(model_phase)
    model_re = lax.dynamic_slice_in_dim(full_re, block_index * row_count, row_count, 1)
    model_im = lax.dynamic_slice_in_dim(full_im, block_index * row_count, row_count, 1)

    def sweep(gain_re, gain_im):
        probe_re = gain_re * model_re - gain_im * model_im
        probe_im = gain_re * model_im + gain_im * model_re
        probes = lax.all_gather(jnp.stack([probe_re, probe_im]), "blk", axis=2, tiled=True)
        power = jnp.sum(probes * probes, axis=(0, 2))
        products = jnp.einsum("rcpq,scq->rscp", correlation, probes, precision=high)
        product_re = products[0, 0] - products[1, 1]
        product_im = products[0, 1] + products[1, 0]
        return update_gains(model_re, model_im, power, product_re, product_im)

    def paired(step_index, carried):
        first_re, first_im = sweep(carried[0], carried[1])
        second_re, second_im = sweep(first_re, first_im)
        return (0.5 * (second_re + first_re), 0.5 * (second_im + first_im))

    start_re = jnp.ones((local_chans, row_count), jnp.float32)
    start_im = jnp.zeros((local_chans, row_count), jnp.float32)
    gain_re, gain_im = lax.fori_loop(0, ITERS // 2, paired, (start_re, start_im))
    solved = lax.all_gather(jnp.stack([gain_re, gain_im]), "blk", axis=2, tiled=True)
    owners = lax.all_to_all(solved, "chan", split_axis=2, concat_axis=1, tiled=True)
    gains = lax.dynamic_slice_in_dim(owners, block_index * input_count, input_count, 2)
    return (visibility, gains)


def solution(mesh):
    return jax.shard_map(
        shards,
        mesh=mesh,
        in_specs=(P(("chan", "blk"), None), P(("chan", "blk")), P("chan", None), P("chan", None)),
        out_specs=(P(None, "chan", "blk", None), P(None, None, ("chan", "blk"))),
        check_vma=False,
    )
```

profile of v0, /device:TPU:1, one launch (start us, length us, event | category | flops | bytes accessed | tf_op | source)
XLA Modules:
  0.0 805.5 jit_solution(235510974840824915)
XLA Ops:
  14.5 10.1 %reshape.358 = f32[16,263,512]{2,1,0:T(8,128)} reshape(f32[16,134656]{1,0:T(8,128)} %convert_element_type.41) | data formatting | bytes 17235968 | tf_op jit(solution)/shard_map/reshape | solution.py:35
  24.6 27.3 %fusion.34 = bf16[128,16,2,256]{3,0,1,2:T(8,128)(2,1)} fusion(f32[16]{0:T(128)S(1)} %convert_multiply_fusion, f32[16,263,512]{2,1,0:T(8,128)} %reshape.358, f32[512]{0:T(512)S(1)} %get-tuple-element.223, f32[512]{0:T(512)S(1)} %get-tuple-element.224, f32[512]{0:T(512)S(1)} %get-tuple-element.225, f32[512]{0:T(512)S(1)} %get-tuple-element.226, ...), kind=kOutput, calls=%fused_computation.70 | convolution fusion | flops 1109917696 | bytes 69484608 | tf_op jit(solution)/shard_map/itj,jrc->cirt/dot_general | solution.py:40
  52.0 66.1 %all-gather.2.cloned.1.call-done = bf16[128,64,2,256]{3,0,1,2:T(8,128)(2,1)} async-done(((bf16[128,16,2,256]{3,0,1,2:T(8,128)(2,1)}), bf16[128,64,2,256]{3,0,1,2:T(8,128)(2,1)}) %all-gather.2.cloned.1.call-update) | async-done | bytes 8388624 | tf_op jit(solution)/shard_map/all_gather | solution.py:58
  118.1 11.5 %copy.43 = bf16[128,64,2,256]{3,1,2,0:T(8,128)(2,1)} copy(bf16[128,64,2,256]{3,0,1,2:T(8,128)(2,1)} %all-gather.2.cloned.1.call-done) | data formatting | bytes 16777216 | tf_op jit(solution)/shard_map/all_gather | solution.py:58
  129.7 7.3 all-to-all-start
  137.8 117.2 %all-to-all-done = bf16[128,64,2,256]{3,1,2,0:T(8,128)(2,1)} async-done(((bf16[128,64,2,256]{3,1,2,0:T(8,128)(2,1)}), bf16[128,64,2,256]{3,1,2,0:T(8,128)(2,1)}, u32[]{:S(2)}, u32[]{:S(2)}) %all-to-all-start) | async-done | bytes 8388640 | tf_op jit(solution)/shard_map/all_to_all | solution.py:59
  254.9 16.4 %copy.81 = bf16[32,4,64,2,256]{4,3,2,0,1:T(2,128)(2,1)} copy(bf16[32,4,64,2,256]{4,2,3,1,0:T(8,128)(2,1)} %bitcast.4) | data formatting | bytes 16777216 | tf_op jit(solution)/shard_map/all_to_all | solution.py:59
  271.4 14.1 %reshape.359 = bf16[4,2048,512]{2,1,0:T(8,128)(2,1)} reshape(bf16[4,32,64,2,256]{4,3,2,1,0:T(2,128)(2,1)} %bitcast.199) | data formatting | bytes 16777216 | tf_op jit(solution)/shard_map/reshape | solution.py:63
  285.4 14.1 %reshape.366 = bf16[4,2048,512,1]{2,1,0,3:T(8,128)(2,1)} reshape(bf16[4,32,64,2,256]{4,3,2,1,0:T(2,128)(2,1)} %bitcast.200) | data formatting | bytes 16777216 | tf_op jit(solution)/shard_map/reshape | solution.py:63
  304.6 22.1 %fusion.78 = (bf16[2,4,512,2048]{2,3,0,1:T(8,128)(2,1)}, f32[2,4,512,2048]{2,3,0,1:T(8,128)}) fusion(bf16[1,4,512,512]{3,2,0,1:T(8,128)(2,1)S(1)} %get-tuple-element.234, bf16[1,4,512,512]{3,2,0,1:T(8,128)(2,1)} %get-tuple-element.235, bf16[4,2048,512,1]{2,1,0,3:T(8,128)(2,1)} %reshape.366), kind=kOutput, calls=%fused_computation.137 | convolution fusion | flops 8615100416 | bytes 62914560 | tf_op jit(solution)/shard_map/rcpk,cqk->rcpq/dot_general | solution.py:68
  326.7 31.8 %copy.45 = f32[2,4,512,2048]{3,2,0,1:T(8,128)} copy(f32[2,4,512,2048]{2,3,0,1:T(8,128)} %get-tuple-element.233) | data formatting | bytes 67108864
  358.5 381.5 %while.16 = (s32[]{:T(128)}, f32[4,512]{1,0:T(4,128)S(1)}, f32[4,512]{1,0:T(4,128)S(1)}, f32[4,512]{1,0:T(4,128)S(1)}, f32[4,512]{1,0:T(4,128)S(1)}, /*index=5*/...) while((s32[]{:T(128)}, f32[4,512]{1,0:T(4,128)S(1)}, ...), condition=%wide.region_3.4_spmd.clone, body=%wide.region_0.3_spmd.clone.sunk | while | flops 402845696 | bytes 68075792 | solution.py:94
  358.6 8.9 %all_gather.24 = f32[2,4,2048]{2,0,1:T(2,128)S(1)} all-gather(f32[2,4,512]{2,0,1:T(2,128)S(1)} %pad_maximum_fusion.5), channel_id=1, replica_groups=mesh['chan'=32,'blk'=4] {'blk'}, dimensions={2}, use_global_device_ids=true | all-gather | bytes 81920 | tf_op jit(solution)/shard_map/while/body/eval_jaxpr/all_gather | solution.py:80
  367.5 30.8 %convolution_bitcast_fusion.2 = f32[2,2,4,512]{3,1,0,2:T(2,128)S(1)} fusion(f32[2,4,512,2048]{3,2,0,1:T(8,128)} %get-tuple-element.328, f32[2,4,2048]{2,0,1:T(2,128)S(1)} %all_gather.24), kind=kOutput, calls=%fused_computation.clone.1 | convolution fusion | flops 201326592 | bytes 33652736 | tf_op jit(solution)/shard_map/while/body/eval_jaxpr/rcpq,scq->rscp/dot_general | solution.py:82
  398.6 6.8 all_gather.25
  405.4 30.8 %fusion.97 = f32[4,2,2,512]{3,1,2,0:T(2,128)S(1)} fusion(f32[2,4,512,2048]{3,2,0,1:T(8,128)} %get-tuple-element.328, f32[2,4,2048,1]{2,1,0,3:T(4,128)S(1)} %bitcast.201), kind=kOutput, calls=%fused_computation.2.clone.1 | convolution fusion | flops 201326592 | bytes 33652736 | tf_op jit(solution)/shard_map/while/body/eval_jaxpr/rcpq,scq->rscp/dot_general | solution.py:82
  436.6 6.8 all_gather.24
  443.3 30.8 %convolution_bitcast_fusion.2 = f32[2,2,4,512]{3,1,0,2:T(2,128)S(1)} fusion(f32[2,4,512,2048]{3,2,0,1:T(8,128)} %get-tuple-element.328, f32[2,4,2048]{2,0,1:T(2,128)S(1)} %all_gather.24), kind=kOutput, calls=%fused_computation.clone.1 | convolution fusion | flops 201326592 | bytes 33652736 | tf_op jit(solution)/shard_map/while/body/eval_jaxpr/rcpq,scq->rscp/dot_general | solution.py:82
  474.5 6.8 all_gather.25
  481.2 30.8 %fusion.97 = f32[4,2,2,512]{3,1,2,0:T(2,128)S(1)} fusion(f32[2,4,512,2048]{3,2,0,1:T(8,128)} %get-tuple-element.328, f32[2,4,2048,1]{2,1,0,3:T(4,128)S(1)} %bitcast.201), kind=kOutput, calls=%fused_computation.2.clone.1 | convolution fusion | flops 201326592 | bytes 33652736 | tf_op jit(solution)/shard_map/while/body/eval_jaxpr/rcpq,scq->rscp/dot_general | solution.py:82
  512.4 6.8 all_gather.24
  519.2 30.8 %convolution_bitcast_fusion.2 = f32[2,2,4,512]{3,1,0,2:T(2,128)S(1)} fusion(f32[2,4,512,2048]{3,2,0,1:T(8,128)} %get-tuple-element.328, f32[2,4,2048]{2,0,1:T(2,128)S(1)} %all_gather.24), kind=kOutput, calls=%fused_computation.clone.1 | convolution fusion | flops 201326592 | bytes 33652736 | tf_op jit(solution)/shard_map/while/body/eval_jaxpr/rcpq,scq->rscp/dot_general | solution.py:82
  550.3 6.8 all_gather.25
  557.0 30.8 %fusion.97 = f32[4,2,2,512]{3,1,2,0:T(2,128)S(1)} fusion(f32[2,4,512,2048]{3,2,0,1:T(8,128)} %get-tuple-element.328, f32[2,4,2048,1]{2,1,0,3:T(4,128)S(1)} %bitcast.201), kind=kOutput, calls=%fused_computation.2.clone.1 | convolution fusion | flops 201326592 | bytes 33652736 | tf_op jit(solution)/shard_map/while/body/eval_jaxpr/rcpq,scq->rscp/dot_general | solution.py:82
  588.2 6.8 all_gather.24
  595.0 30.8 %convolution_bitcast_fusion.2 = f32[2,2,4,512]{3,1,0,2:T(2,128)S(1)} fusion(f32[2,4,512,2048]{3,2,0,1:T(8,128)} %get-tuple-element.328, f32[2,4,2048]{2,0,1:T(2,128)S(1)} %all_gather.24), kind=kOutput, calls=%fused_computation.clone.1 | convolution fusion | flops 201326592 | bytes 33652736 | tf_op jit(solution)/shard_map/while/body/eval_jaxpr/rcpq,scq->rscp/dot_general | solution.py:82
  626.1 6.8 all_gather.25
  632.9 30.8 %fusion.97 = f32[4,2,2,512]{3,1,2,0:T(2,128)S(1)} fusion(f32[2,4,512,2048]{3,2,0,1:T(8,128)} %get-tuple-element.328, f32[2,4,2048,1]{2,1,0,3:T(4,128)S(1)} %bitcast.201), kind=kOutput, calls=%fused_computation.2.clone.1 | convolution fusion | flops 201326592 | bytes 33652736 | tf_op jit(solution)/shard_map/while/body/eval_jaxpr/rcpq,scq->rscp/dot_general | solution.py:82
  670.8 30.8 %convolution_bitcast_fusion.2 = f32[2,2,4,512]{3,1,0,2:T(2,128)S(1)} fusion(f32[2,4,512,2048]{3,2,0,1:T(8,128)} %get-tuple-element.328, f32[2,4,2048]{2,0,1:T(2,128)S(1)} %all_gather.24), kind=kOutput, calls=%fused_computation.clone.1 | convolution fusion | flops 201326592 | bytes 33652736 | tf_op jit(solution)/shard_map/while/body/eval_jaxpr/rcpq,scq->rscp/dot_general | solution.py:82
  708.7 30.8 %fusion.97 = f32[4,2,2,512]{3,1,2,0:T(2,128)S(1)} fusion(f32[2,4,512,2048]{3,2,0,1:T(8,128)} %get-tuple-element.328, f32[2,4,2048,1]{2,1,0,3:T(4,128)S(1)} %bitcast.201), kind=kOutput, calls=%fused_computation.2.clone.1 | convolution fusion | flops 201326592 | bytes 33652736 | tf_op jit(solution)/shard_map/while/body/eval_jaxpr/rcpq,scq->rscp/dot_general | solution.py:82
  751.7 18.3 %all-to-all-start.1 = ((f32[32,1,512]{2,1,0:T(1,128)}), f32[32,1,512]{2,1,0:T(1,128)S(1)}, u32[]{:S(2)}, u32[]{:S(2)}) async-start(f32[32,1,512]{2,1,0:T(1,128)} %reshape.368), calls=%async_computation.1 | async-start | bytes 131072 | tf_op jit(solution)/shard_map/all_to_all | solution.py:96
  770.0 21.5 %copy.48 = bf16[2,4,512,2048]{3,2,1,0:T(8,128)(2,1)} copy(bf16[2,4,512,2048]{2,3,0,1:T(8,128)(2,1)} %get-tuple-element.232) | data formatting | bytes 33554432
  (98 shorter events, 48.8 us)
Async XLA Ops:
  7.2 111.0 %all-gather.2.cloned.1.call-start = ((), (), s32[]{:S(2)}) async-start(), calls=%async_computation.2 | async-start | bytes 10485760 | tf_op jit(solution)/shard_map/all_gather | solution.py:58
  14.5 10.2 %copy-start = (s32[16]{0:T(128)S(1)}, s32[16]{0:T(128)}, u32[]{:S(2)}) copy-start(s32[16]{0:T(128)} %param.7) | copy-start | bytes 196
  129.7 125.3 %all-to-all-start = ((bf16[128,64,2,256]{3,1,2,0:T(8,128)(2,1)}), bf16[128,64,2,256]{3,1,2,0:T(8,128)(2,1)}, u32[]{:S(2)}, u32[]{:S(2)}) async-start(bf16[128,64,2,256]{3,1,2,0:T(8,128)(2,1)} %copy.43), calls=%async_computation | async-start | bytes 16777216 | tf_op jit(solution)/shard_map/all_to_all | solution.py:59
  751.7 39.8 %all-to-all-start.1 = ((f32[32,1,512]{2,1,0:T(1,128)}), f32[32,1,512]{2,1,0:T(1,128)S(1)}, u32[]{:S(2)}, u32[]{:S(2)}) async-start(f32[32,1,512]{2,1,0:T(1,128)} %reshape.368), calls=%async_computation.1 | async-start | bytes 131072 | tf_op jit(solution)/shard_map/all_to_all | solution.py:96
Sparse Core Ops, SparseCore 0:
  52.1 65.9 all-gather.1
where the time goes:
time: 808 us; the launch traced here: 806 us
  matrix products  357 us (44%)
  waiting for transfers between devices  183 us (23%)
  local copies, waits for them, and re-layouts  131 us (16%)
  blocking collectives  76.4 us (9%)
  starting transfers between devices  25.6 us (3%)
  other arithmetic  17 us (2%)
  between operations  14.2 us (2%)
    dot_general x10, matrix products, sweep(): products = jnp.einsum('rcpq,scq->rscp', correlation, probes, precision=high)  308 us
    all_to_all x1, waiting for transfers between devices, shards(): lax.all_to_all(grouped, 'chan', split_axis=0, concat_axis=1, tiled=True)  117 us
    all_gather x10, blocking collectives, sweep(): lax.all_gather(jnp.stack([probe_re, probe_im]), 'blk', axis=2, tiled=True)  69.7 us
    all_gather x1, waiting for transfers between devices, shards(): grouped = lax.all_gather(spectra, 'blk', axis=1, tiled=True)  66.1 us
    unnamed x7, local copies, waits for them, and re-layouts  61 us
    reshape x2, local copies, waits for them, and re-layouts, shards(): whole = turned.reshape(local_chans, all_inputs, 2 * SPECTRA)  28.1 us
    dot_general x1, matrix products, channelize(): jnp.einsum('itj,jrc->cirt', frames, table, preferred_element_type=jnp.flo...  27.3 us
    dot_general x1, matrix products, shards(): jnp.einsum('rcpk,cqk->rcpq', stacked, whole, preferred_element_type=jnp.f...  22.1 us
  transfers between devices with their start and end apart: 3, of which 2 were waited for; matrix products, arithmetic and copies ran while one was open for 3% of the time, Pallas kernels for 0%

commit v1 on v0

--- a/solution.py
+++ b/solution.py
@@ -56,7 +56,16 @@
     blk_count = lax.axis_size("blk")
     block_index = lax.axis_index("blk")
     grouped = lax.all_gather(spectra, "blk", axis=1, tiled=True)
-    turned = lax.all_to_all(grouped, "chan", split_axis=0, concat_axis=1, tiled=True)
+    _produce_grid = lambda mine_x, dimension_no, at_axis: jnp.concatenate(
+        lax.all_to_all(
+            jnp.stack(jnp.split(mine_x, lax.axis_size("chan"), axis=dimension_no)),
+            axis_name="chan",
+            split_axis=0,
+            concat_axis=0,
+        ),
+        axis=at_axis,
+    )
+    turned = _produce_grid(grouped, 0, 1)
     local_chans = turned.shape[0]
     all_inputs = turned.shape[1]
     row_count = all_inputs // blk_count

time: 808 us -> 857 us (1.061)
  local copies, waits for them, and re-layouts: 131 us -> 178 us
    unnamed x7 -> x38, local copies, waits for them, and re-layouts: 61 us -> 118 us
    another operation x0 -> x3, local copies, waits for them, and re-layouts: none -> 30 us  [the longest x2 28.1 us: shards(): whole = turned.reshape(local_chans, all_inputs, 2 * SPECTRA)]
    all_to_all x1 -> x0, local copies, waits for them, and re-layouts: 16.4 us -> none  [shards(): lax.all_to_all(grouped, 'chan', split_axis=0, concat_axis=1, tiled=True)]
    reshape x2 -> x1, local copies, waits for them, and re-layouts: 28.1 us -> 16.3 us  [shards(): jnp.concatenate(lax.all_to_all(jnp.stack(jnp.split(mine_x, lax.axis_size(...]
    all_gather x1 -> x0, local copies, waits for them, and re-layouts: 11.5 us -> none  [shards(): grouped = lax.all_gather(spectra, 'blk', axis=1, tiled=True)]
where the time goes in v1:
time: 857 us; the launch traced here: 853 us
  matrix products  357 us (42%)
  waiting for transfers between devices  183 us (21%)
  local copies, waits for them, and re-layouts  178 us (21%)
  blocking collectives  76.4 us (9%)
  starting transfers between devices  25.6 us (3%)
  other arithmetic  17 us (2%)
  between operations  14.2 us (2%)
    dot_general x10, matrix products, sweep(): products = jnp.einsum('rcpq,scq->rscp', correlation, probes, precision=high)  308 us
    unnamed x38, local copies, waits for them, and re-layouts  118 us
    all_to_all x1, waiting for transfers between devices, shards(): lax.all_to_all(jnp.stack(jnp.split(mine_x, lax.axis_size('chan'), axis=di...  117 us
    all_gather x10, blocking collectives, sweep(): lax.all_gather(jnp.stack([probe_re, probe_im]), 'blk', axis=2, tiled=True)  69.7 us
    all_gather x1, waiting for transfers between devices, shards(): grouped = lax.all_gather(spectra, 'blk', axis=1, tiled=True)  66.1 us
    another operation x2, local copies, waits for them, and re-layouts, shards(): whole = turned.reshape(local_chans, all_inputs, 2 * SPECTRA)  28.1 us
    dot_general x1, matrix products, channelize(): jnp.einsum('itj,jrc->cirt', frames, table, preferred_element_type=jnp.flo...  27.3 us
    dot_general x1, matrix products, shards(): jnp.einsum('rcpk,cqk->rcpq', stacked, whole, preferred_element_type=jnp.f...  22.1 us
  transfers between devices with their start and end apart: 3, of which 2 were waited for; matrix products, arithmetic and copies ran while one was open for 3% of the time, Pallas kernels for 0%

profile of v1, /device:TPU:1, one launch (start us, length us, event | category | flops | bytes accessed | tf_op | source)
XLA Modules:
  0.0 853.0 jit_solution(15456298881398994020)
XLA Ops:
  14.5 10.1 %reshape.357 = f32[16,263,512]{2,1,0:T(8,128)} reshape(f32[16,134656]{1,0:T(8,128)} %convert_element_type.41) | data formatting | bytes 17235968 | tf_op jit(solution)/shard_map/reshape | solution.py:35
  24.6 27.3 %fusion.34 = bf16[128,16,2,256]{3,0,1,2:T(8,128)(2,1)} fusion(f32[16]{0:T(128)S(1)} %convert_multiply_fusion, f32[16,263,512]{2,1,0:T(8,128)} %reshape.357, f32[512]{0:T(512)S(1)} %get-tuple-element.223, f32[512]{0:T(512)S(1)} %get-tuple-element.224, f32[512]{0:T(512)S(1)} %get-tuple-element.225, f32[512]{0:T(512)S(1)} %get-tuple-element.226, ...), kind=kOutput, calls=%fused_computation.69 | convolution fusion | flops 1109917696 | bytes 69484608 | tf_op jit(solution)/shard_map/itj,jrc->cirt/dot_general | solution.py:40
  52.0 66.1 %all-gather.2.cloned.1.call-done = bf16[128,64,2,256]{3,0,1,2:T(8,128)(2,1)} async-done(((bf16[128,16,2,256]{3,0,1,2:T(8,128)(2,1)}), bf16[128,64,2,256]{3,0,1,2:T(8,128)(2,1)}) %all-gather.2.cloned.1.call-update) | async-done | bytes 8388624 | tf_op jit(solution)/shard_map/all_gather | solution.py:58
  177.2 7.3 all-to-all-start
  185.4 117.2 %all-to-all-done = bf16[32,4,64,2,256]{4,1,2,3,0:T(4,128)(2,1)} async-done(((bf16[32,4,64,2,256]{4,1,2,3,0:T(4,128)(2,1)}), bf16[32,4,64,2,256]{4,1,2,3,0:T(4,128)(2,1)}, u32[]{:S(2)}, u32[]{:S(2)}) %all-to-all-start) | async-done | bytes 8388640 | tf_op jit(solution)/shard_map/all_to_all | solution.py:60
  302.5 16.3 %copy.41 = bf16[4,32,64,2,256]{4,3,2,1,0:T(2,128)(2,1)} copy(bf16[4,32,64,2,256]{4,0,2,3,1:T(4,128)(2,1)} %bitcast.36) | data formatting | bytes 16777216 | tf_op jit(solution)/shard_map/reshape | solution.py:59
  318.8 14.1 %reshape_reshape.3 = bf16[4,2048,512]{2,1,0:T(8,128)(2,1)} reshape(bf16[4,32,64,2,256]{4,3,2,1,0:T(2,128)(2,1)} %copy.41) | data formatting | bytes 16777216 | tf_op jit(solution)/shard_map/reshape;reshape | solution.py:72
  332.9 14.1 %reshape.365 = bf16[4,2048,512,1]{2,1,0,3:T(8,128)(2,1)} reshape(bf16[4,32,64,2,256]{4,3,2,1,0:T(2,128)(2,1)} %copy.41) | data formatting | bytes 16777216 | tf_op jit(solution)/shard_map/reshape;reshape | solution.py:72
  352.1 22.1 %fusion.110 = (bf16[2,4,512,2048]{2,3,0,1:T(8,128)(2,1)}, f32[2,4,512,2048]{2,3,0,1:T(8,128)}) fusion(bf16[1,4,512,512]{3,2,0,1:T(8,128)(2,1)S(1)} %get-tuple-element.234, bf16[1,4,512,512]{3,2,0,1:T(8,128)(2,1)} %get-tuple-element.235, bf16[4,2048,512,1]{2,1,0,3:T(8,128)(2,1)} %reshape.365), kind=kOutput, calls=%fused_computation.200 | convolution fusion | flops 8615100416 | bytes 62914560 | tf_op jit(solution)/shard_map/rcpk,cqk->rcpq/dot_general | solution.py:77
  374.2 31.8 %copy.42 = f32[2,4,512,2048]{3,2,0,1:T(8,128)} copy(f32[2,4,512,2048]{2,3,0,1:T(8,128)} %get-tuple-element.233) | data formatting | bytes 67108864
  406.0 381.5 %while.16 = (s32[]{:T(128)}, f32[4,512]{1,0:T(4,128)S(1)}, f32[4,512]{1,0:T(4,128)S(1)}, f32[4,512]{1,0:T(4,128)S(1)}, f32[4,512]{1,0:T(4,128)S(1)}, /*index=5*/...) while((s32[]{:T(128)}, f32[4,512]{1,0:T(4,128)S(1)}, ...), condition=%wide.region_3.4_spmd.clone, body=%wide.region_0.3_spmd.clone.sunk | while | flops 402845696 | bytes 68075792 | solution.py:103
  406.0 8.9 %all_gather.24 = f32[2,4,2048]{2,0,1:T(2,128)S(1)} all-gather(f32[2,4,512]{2,0,1:T(2,128)S(1)} %pad_maximum_fusion.5), channel_id=1, replica_groups=mesh['chan'=32,'blk'=4] {'blk'}, dimensions={2}, use_global_device_ids=true | all-gather | bytes 81920 | tf_op jit(solution)/shard_map/while/body/eval_jaxpr/all_gather | solution.py:89
  415.0 30.8 %convolution_bitcast_fusion.2 = f32[2,2,4,512]{3,1,0,2:T(2,128)S(1)} fusion(f32[2,4,512,2048]{3,2,0,1:T(8,128)} %get-tuple-element.328, f32[2,4,2048]{2,0,1:T(2,128)S(1)} %all_gather.24), kind=kOutput, calls=%fused_computation.clone.1 | convolution fusion | flops 201326592 | bytes 33652736 | tf_op jit(solution)/shard_map/while/body/eval_jaxpr/rcpq,scq->rscp/dot_general | solution.py:91
  446.1 6.8 all_gather.25
  452.8 30.8 %fusion.129 = f32[4,2,2,512]{3,1,2,0:T(2,128)S(1)} fusion(f32[2,4,512,2048]{3,2,0,1:T(8,128)} %get-tuple-element.328, f32[2,4,2048,1]{2,1,0,3:T(4,128)S(1)} %bitcast.324), kind=kOutput, calls=%fused_computation.2.clone.1 | convolution fusion | flops 201326592 | bytes 33652736 | tf_op jit(solution)/shard_map/while/body/eval_jaxpr/rcpq,scq->rscp/dot_general | solution.py:91
  484.0 6.8 all_gather.24
  490.8 30.8 %convolution_bitcast_fusion.2 = f32[2,2,4,512]{3,1,0,2:T(2,128)S(1)} fusion(f32[2,4,512,2048]{3,2,0,1:T(8,128)} %get-tuple-element.328, f32[2,4,2048]{2,0,1:T(2,128)S(1)} %all_gather.24), kind=kOutput, calls=%fused_computation.clone.1 | convolution fusion | flops 201326592 | bytes 33652736 | tf_op jit(solution)/shard_map/while/body/eval_jaxpr/rcpq,scq->rscp/dot_general | solution.py:91
  521.9 6.8 all_gather.25
  528.7 30.8 %fusion.129 = f32[4,2,2,512]{3,1,2,0:T(2,128)S(1)} fusion(f32[2,4,512,2048]{3,2,0,1:T(8,128)} %get-tuple-element.328, f32[2,4,2048,1]{2,1,0,3:T(4,128)S(1)} %bitcast.324), kind=kOutput, calls=%fused_computation.2.clone.1 | convolution fusion | flops 201326592 | bytes 33652736 | tf_op jit(solution)/shard_map/while/body/eval_jaxpr/rcpq,scq->rscp/dot_general | solution.py:91
  559.9 6.8 all_gather.24
  566.6 30.8 %convolution_bitcast_fusion.2 = f32[2,2,4,512]{3,1,0,2:T(2,128)S(1)} fusion(f32[2,4,512,2048]{3,2,0,1:T(8,128)} %get-tuple-element.328, f32[2,4,2048]{2,0,1:T(2,128)S(1)} %all_gather.24), kind=kOutput, calls=%fused_computation.clone.1 | convolution fusion | flops 201326592 | bytes 33652736 | tf_op jit(solution)/shard_map/while/body/eval_jaxpr/rcpq,scq->rscp/dot_general | solution.py:91
  597.7 6.8 all_gather.25
  604.5 30.8 %fusion.129 = f32[4,2,2,512]{3,1,2,0:T(2,128)S(1)} fusion(f32[2,4,512,2048]{3,2,0,1:T(8,128)} %get-tuple-element.328, f32[2,4,2048,1]{2,1,0,3:T(4,128)S(1)} %bitcast.324), kind=kOutput, calls=%fused_computation.2.clone.1 | convolution fusion | flops 201326592 | bytes 33652736 | tf_op jit(solution)/shard_map/while/body/eval_jaxpr/rcpq,scq->rscp/dot_general | solution.py:91
  635.7 6.8 all_gather.24
  642.4 30.8 %convolution_bitcast_fusion.2 = f32[2,2,4,512]{3,1,0,2:T(2,128)S(1)} fusion(f32[2,4,512,2048]{3,2,0,1:T(8,128)} %get-tuple-element.328, f32[2,4,2048]{2,0,1:T(2,128)S(1)} %all_gather.24), kind=kOutput, calls=%fused_computation.clone.1 | convolution fusion | flops 201326592 | bytes 33652736 | tf_op jit(solution)/shard_map/while/body/eval_jaxpr/rcpq,scq->rscp/dot_general | solution.py:91
  673.6 6.8 all_gather.25
  680.3 30.8 %fusion.129 = f32[4,2,2,512]{3,1,2,0:T(2,128)S(1)} fusion(f32[2,4,512,2048]{3,2,0,1:T(8,128)} %get-tuple-element.328, f32[2,4,2048,1]{2,1,0,3:T(4,128)S(1)} %bitcast.324), kind=kOutput, calls=%fused_computation.2.clone.1 | convolution fusion | flops 201326592 | bytes 33652736 | tf_op jit(solution)/shard_map/while/body/eval_jaxpr/rcpq,scq->rscp/dot_general | solution.py:91
  711.5 6.8 all_gather.24
  718.3 30.8 %convolution_bitcast_fusion.2 = f32[2,2,4,512]{3,1,0,2:T(2,128)S(1)} fusion(f32[2,4,512,2048]{3,2,0,1:T(8,128)} %get-tuple-element.328, f32[2,4,2048]{2,0,1:T(2,128)S(1)} %all_gather.24), kind=kOutput, calls=%fused_computation.clone.1 | convolution fusion | flops 201326592 | bytes 33652736 | tf_op jit(solution)/shard_map/while/body/eval_jaxpr/rcpq,scq->rscp/dot_general | solution.py:91
  756.1 30.8 %fusion.129 = f32[4,2,2,512]{3,1,2,0:T(2,128)S(1)} fusion(f32[2,4,512,2048]{3,2,0,1:T(8,128)} %get-tuple-element.328, f32[2,4,2048,1]{2,1,0,3:T(4,128)S(1)} %bitcast.324), kind=kOutput, calls=%fused_computation.2.clone.1 | convolution fusion | flops 201326592 | bytes 33652736 | tf_op jit(solution)/shard_map/while/body/eval_jaxpr/rcpq,scq->rscp/dot_general | solution.py:91
  799.1 18.3 %all-to-all-start.1 = ((f32[32,1,512]{2,1,0:T(1,128)}), f32[32,1,512]{2,1,0:T(1,128)S(1)}, u32[]{:S(2)}, u32[]{:S(2)}) async-start(f32[32,1,512]{2,1,0:T(1,128)} %reshape.367), calls=%async_computation.1 | async-start | bytes 131072 | tf_op jit(solution)/shard_map/all_to_all | solution.py:105
  817.4 21.5 %copy.45 = bf16[2,4,512,2048]{3,2,1,0:T(8,128)(2,1)} copy(bf16[2,4,512,2048]{2,3,0,1:T(8,128)(2,1)} %get-tuple-element.232) | data formatting | bytes 33554432
  (129 shorter events, 101.1 us)
Async XLA Ops:
  7.2 111.0 %all-gather.2.cloned.1.call-start = ((), (), s32[]{:S(2)}) async-start(), calls=%async_computation.2 | async-start | bytes 10485760 | tf_op jit(solution)/shard_map/all_gather | solution.py:58
  14.5 10.2 %copy-start = (s32[16]{0:T(128)S(1)}, s32[16]{0:T(128)}, u32[]{:S(2)}) copy-start(s32[16]{0:T(128)} %param.7) | copy-start | bytes 196
  177.2 125.3 %all-to-all-start = ((bf16[32,4,64,2,256]{4,1,2,3,0:T(4,128)(2,1)}), bf16[32,4,64,2,256]{4,1,2,3,0:T(4,128)(2,1)}, u32[]{:S(2)}, u32[]{:S(2)}) async-start(bf16[32,4,64,2,256]{4,1,2,3,0:T(4,128)(2,1)} %fusion.40), calls=%async_computation | async-start | bytes 16777216 | tf_op jit(solution)/shard_map/all_to_all | solution.py:60
  799.1 39.8 %all-to-all-start.1 = ((f32[32,1,512]{2,1,0:T(1,128)}), f32[32,1,512]{2,1,0:T(1,128)S(1)}, u32[]{:S(2)}, u32[]{:S(2)}) async-start(f32[32,1,512]{2,1,0:T(1,128)} %reshape.367), calls=%async_computation.1 | async-start | bytes 131072 | tf_op jit(solution)/shard_map/all_to_all | solution.py:105
Sparse Core Ops, SparseCore 0:
  52.1 65.9 all-gather.1
